TPU v7x, 32 devices: a whole 2x2x4 slice. The times are simulated.
32 devices in a mesh: wave: 4 (over z), lev: 8 (over y, x, core).
Axes of the slice: x: 2, y: 2, z: 4, core: 2. Of those that a mesh axis runs over, the one named last changes fastest.
Arguments:
- spec: bfloat16 [1280, 2, 16, 1280], P('wave', None, 'lev'), may hold values from -0.119628906 to 0.119628906
- legendre: bfloat16 [1280, 16, 1280], P(('wave', 'lev')), may hold values from -0.15625 to 0.15625
- slot_wave: int32 [1280], replicated, may hold values from 0 to 1280, as said below
- row_lons: int32 [32], replicated, may hold values from 20 to 5136, as said below
- band_rows: int32 [32], replicated, may hold values from 0 to 31, as said below
Outputs:
- grid: float32 [32, 16, 5136], P('wave', 'lev')
Inputs may be any that keep to these rules, and one draw needn't show every extreme that they name: `slot_wave`: every zonal wavenumber 0 to 1279 stands in exactly one slot; any other slot holds 1280. `row_lons`: row 16 + j has as many points as row j; each count is 20 plus a multiple of 4; some row has 5136. `band_rows`: a permutation of the latitude rows.
All inputs are finite; a program needn't handle non-finite values.
Results may differ from a plain program's by a relative error of at most 0.0037.
Values may be sent and summed in bfloat16 or wider, within the bound.
No kernel may reach another device: no remote copies, remote signals or barrier semaphores. Data moves between devices by JAX's collectives and lax.ppermute only.
A program may use at most 64 MiB of HBM per device.

v0:
```python
import math
import jax
import jax.numpy as jnp
import numpy as np
from jax import lax
from jax.sharding import Mesh
from jax.sharding import PartitionSpec as P


def angles(remainder, points):
    return 2.0 * math.pi * remainder.astype(jnp.float32) / points.astype(jnp.float32)


def trig_pair(step, lon_idx, points, count):
    mult = jnp.arange(count, dtype=jnp.int32)[:, None] * step
    theta = angles(mult * lon_idx[None, :] % points, points)
    return (jnp.cos(theta), jnp.sin(theta))


def compose(first, second):
    c0, s0 = first
    c1, s1 = second
    cos = c1[:, None] * c0[None] - s1[:, None] * s0[None]
    sin = s1[:, None] * c0[None] + c1[:, None] * s0[None]
    return (cos.reshape(-1, cos.shape[-1]), sin.reshape(-1, sin.shape[-1]))


def row_synthesis(coef_row, points):
    fields = coef_row.shape[1]
    waves = coef_row.shape[2]
    ablocks = waves // 64
    lon_len = 20 + 4 * (waves - 1)
    lon_idx = jnp.arange(lon_len, dtype=jnp.int32)
    cos_t, sin_t = compose(trig_pair(1, lon_idx, points, 8), trig_pair(8, lon_idx, points, 8))
    cosb = cos_t.astype(jnp.bfloat16)
    sinb = sin_t.astype(jnp.bfloat16)
    n_a1 = -(-ablocks // 4)
    cosp, sinp = compose(trig_pair(64, lon_idx, points, 4), trig_pair(256, lon_idx, points, n_a1))
    cosp = cosp[:ablocks]
    sinp = sinp[:ablocks]
    blocks = coef_row.reshape(2, fields, ablocks, 64)
    c0 = blocks[0]
    c1 = blocks[1]
    lhs = jnp.stack([jnp.concatenate([c0, -c1], -1), jnp.concatenate([c1, c0], -1)], 0)
    rhs = jnp.concatenate([cosb, sinb], 0)
    part = jnp.einsum("dfab,bi->dfai", lhs, rhs, preferred_element_type=jnp.float32)
    total = jnp.sum(part[0] * cosp[None] - part[1] * sinp[None], axis=1)
    return jnp.where(lon_idx[None, :] < points, total, jnp.zeros_like(total))


def on_device(spec, legendre, slot_wave, row_lons, band_rows, rows_per_dev):
    n_wave = lax.axis_size("wave")
    n_g = lax.axis_size("lev_g")
    n_r = lax.axis_size("lev_r")
    n_lev = n_g * n_r
    per_dev = legendre.shape[0]
    nlath = legendre.shape[1]
    waves = spec.shape[-1]
    trunc_top = waves - 1
    lev_idx = lax.axis_index("lev_g") * n_r + lax.axis_index("lev_r")
    spec_v = spec.reshape((n_lev, per_dev) + spec.shape[1:])
    gathered = lax.all_to_all(spec_v, ("lev_g", "lev_r"), split_axis=0, concat_axis=0, tiled=True)
    fields = gathered.shape[3] * n_lev
    first_slot = (lax.axis_index("wave") * n_lev + lev_idx) * per_dev
    my_waves = lax.dynamic_slice_in_dim(slot_wave, first_slot, per_dev)
    degree = jnp.arange(waves, dtype=jnp.int32)
    live_k = degree[None, :] <= trunc_top - my_waves[:, None]
    even_mask = (live_k & (degree[None, :] % 2 == 0))[:, None, :]
    odd_mask = (live_k & (degree[None, :] % 2 == 1))[:, None, :]
    zeros = jnp.zeros_like(legendre)
    leg2 = jnp.concatenate(
        [jnp.where(even_mask, legendre, zeros), jnp.where(odd_mask, legendre, zeros)], 1
    )
    sums = jnp.einsum("lscfk,sjk->sclfj", gathered, leg2, preferred_element_type=jnp.float32)
    sums = sums.reshape(per_dev, 2, fields, 2 * nlath)
    north = band_rows < nlath
    lat_idx = jnp.where(north, band_rows, band_rows - nlath)
    j2 = jnp.arange(2 * nlath, dtype=jnp.int32)[:, None]
    sel = jnp.where(j2 == lat_idx[None, :], 1.0, 0.0) + jnp.where(
        j2 == nlath + lat_idx[None, :], jnp.where(north, 1.0, -1.0)[None, :], 0.0
    )
    fourier = jnp.einsum(
        "scfj,jp->scfp",
        sums,
        sel,
        precision=lax.Precision.HIGHEST,
        preferred_element_type=jnp.float32,
    ).astype(jnp.bfloat16)
    rows = band_rows.shape[0]
    fpg = fields // n_g
    fourier = fourier.reshape(per_dev, 2, n_g, fpg, n_wave, n_r, rows_per_dev)
    fourier = jnp.transpose(fourier, (4, 2, 5, 1, 3, 6, 0))
    fourier = fourier.reshape(n_wave * n_g * n_r, 2, fpg, rows_per_dev, per_dev)
    banded = lax.all_to_all(
        fourier, ("wave", "lev_g", "lev_r"), split_axis=0, concat_axis=0, tiled=True
    )
    banded = jnp.transpose(banded, (1, 2, 3, 0, 4)).reshape(2, fpg, rows_per_dev, -1)
    wave_idx = jnp.arange(waves, dtype=jnp.int32)
    first_row = (lax.axis_index("wave") * n_r + lax.axis_index("lev_r")) * rows_per_dev
    my_rows = lax.dynamic_slice_in_dim(band_rows, first_row, rows_per_dev)
    row_points = row_lons[my_rows]
    keep = 2 * wave_idx[None, :] < row_points[:, None]
    factor = jnp.where(keep, jnp.where(wave_idx[None, :] == 0, 2.0, 4.0), 0.0) / 2.0
    onehot = jnp.where(
        slot_wave[None, :, None] == wave_idx[None, None, :], factor[:, None, :], 0.0
    ).astype(jnp.bfloat16)
    coef = jnp.einsum("cfrs,rsm->cfrm", banded, onehot, preferred_element_type=jnp.float32)
    coef = coef.astype(jnp.bfloat16)
    coef_rows = jnp.moveaxis(coef, 2, 0)
    if rows_per_dev == 1:
        grid = row_synthesis(coef_rows[0], row_points[0])[None]
    else:
        grid = lax.map(lambda item: row_synthesis(item[0], item[1]), (coef_rows, row_points))
    lon = grid.shape[-1]
    fpd = fpg // n_r
    grid = grid.reshape(rows_per_dev, n_r, fpd, lon)
    grid = lax.all_to_all(grid, "lev_r", split_axis=1, concat_axis=0, tiled=True)
    return grid.reshape(n_r * rows_per_dev, fpd, lon)


def solution(mesh):

    def run(spec, legendre, slot_wave, row_lons, band_rows):
        n_wave = mesh.shape["wave"]
        n_lev = mesh.shape["lev"]
        rows_w = band_rows.shape[0] // n_wave
        if n_lev >= rows_w:
            n_r = rows_w
            rows_per_dev = 1
        else:
            n_r = n_lev
            rows_per_dev = rows_w // n_lev
        n_g = n_lev // n_r
        devs = np.asarray(mesh.devices).reshape(n_wave, n_g, n_r)
        mesh2 = Mesh(devs, ("wave", "lev_g", "lev_r"))
        lev = ("lev_g", "lev_r")
        fn = jax.shard_map(
            lambda *a: on_device(*a, rows_per_dev=rows_per_dev),
            mesh=mesh2,
            in_specs=(P("wave", None, lev, None), P(("wave",) + lev, None, None), P(), P(), P()),
            out_specs=P("wave", lev, None),
            check_vma=False,
        )
        return fn(spec, legendre, slot_wave, row_lons, band_rows)

    return run
```

profile of v0, /device:TPU:0, one launch (start us, length us, event | category | flops | bytes accessed | tf_op | source)
XLA Modules:
  0.0 82.8 jit_solution(6043936887507259313)
XLA Ops:
  0.0 0.0 copy-start.11
  0.0 0.0 copy-start.10
  0.0 5.3 %all-to-all-start = ((bf16[8,40,2,2,1280]{4,3,2,1,0:T(2,128)(2,1)}), bf16[8,40,2,2,1280]{4,3,2,1,0:T(2,128)(2,1)S(1)}, u32[]{:S(2)}, u32[]{:S(2)}) async-start(bf16[8,40,2,2,1280]{4,3,2,1,0:T(2,128)(2,1)} %bitcast.81), calls=%async_computation | async-start | bytes 6553600 | tf_op jit(solution)/shard_map/all_to_all | solution.py:62
  5.3 0.0 copy-done.11
  5.4 0.6 dynamic_slice.6
  7.9 0.0 copy-done.10
  7.9 0.6 dynamic-slice.2
  10.4 2.9 %fusion.61 = (f32[8,5136]{1,0:T(8,128)S(1)}, f32[8,5136]{1,0:T(8,128)}) fusion(f32[]{:T(128)S(6)} %convert_element_type.83, pred[]{:T(512)S(6)} %lt.109, s32[]{:T(128)S(6)} %select_n.155), kind=kLoop, calls=%fused_computation.79 | loop fusion | flops 451968 | bytes 328713 | tf_op jit(solution)/shard_map/sin | solution.py:17
  13.4 3.1 %fusion.64 = (f32[8,5136]{1,0:T(8,128)}, f32[8,5136]{1,0:T(8,128)}) fusion(f32[]{:T(128)S(6)} %convert_element_type.83, pred[]{:T(512)S(6)} %lt.109, s32[]{:T(128)S(6)} %select_n.155, s32[8]{0:T(128)S(1)} %iota_multiply_fusion.2), kind=kLoop, calls=%fused_computation.82 | loop fusion | flops 451968 | bytes 328745 | tf_op jit(solution)/shard_map/cos | solution.py:17
  16.4 3.0 %fusion.60 = (f32[5,5136]{1,0:T(8,128)}, f32[5,5136]{1,0:T(8,128)}) fusion(f32[]{:T(128)S(6)} %convert_element_type.83, pred[]{:T(512)S(6)} %lt.109, s32[]{:T(128)S(6)} %select_n.155, s32[5]{0:T(128)S(1)} %iota_multiply_fusion.1), kind=kLoop, calls=%fused_computation.78 | loop fusion | flops 282480 | bytes 205469 | tf_op jit(solution)/shard_map/cos | solution.py:17
  19.5 3.0 %fusion.66 = (f32[4,5136]{1,0:T(4,128)S(1)}, f32[4,5136]{1,0:T(4,128)}) fusion(f32[]{:T(128)S(6)} %convert_element_type.83, pred[]{:T(512)S(6)} %lt.109, s32[]{:T(128)S(6)} %select_n.155, s32[4]{0:T(128)S(1)} %iota_multiply_fusion), kind=kLoop, calls=%fused_computation.84 | loop fusion | flops 225984 | bytes 164377 | tf_op jit(solution)/shard_map/cos | solution.py:17
  22.4 0.0 copy-start.6
  22.4 0.0 copy-start.7
  22.4 0.0 copy-start.8
  22.4 0.8 dynamic-slice_subtract_fusion
  23.3 0.1 fusion.27
  23.4 0.0 copy-start.3
  23.4 0.0 copy-start.4
  23.4 0.0 copy-start.5
  23.4 3.6 %broadcast_select_fusion.1 = (bf16[40,16,1280]{2,1,0:T(8,128)(2,1)}, bf16[40,16,1280]{2,1,0:T(8,128)(2,1)}) fusion(bf16[40,16,1280]{2,1,0:T(8,128)(2,1)} %param.6, pred[40,1280]{1,0:T(8,128)(4,1)S(1)} %get-tuple-element.32, pred[40,1280]{1,0:T(8,128)(4,1)S(1)} %get-tuple-element.33), kind=kLoop, calls=%fused_computation.18 | loop fusion | flops 1638400 | bytes 5017600 | tf_op jit(solution)/shard_map/jit(_where)/select_n | solution.py:72
  27.1 0.0 copy-done.6
  27.1 0.0 copy-done.7
  27.1 0.0 copy-done.8
  27.1 1.1 %multiply_subtract_fusion = (f32[5,4,5136]{2,1,0:T(4,128)}, f32[5,4,5136]{2,1,0:T(4,128)}) fusion(f32[4,5136]{1,0:T(4,128)S(1)} %copy-done.8, f32[5,5136]{1,0:T(8,128)S(1)} %copy-done.7, f32[4,5136]{1,0:T(4,128)S(1)} %get-tuple-element.28, f32[5,5136]{1,0:T(8,128)S(1)} %copy-done.6), kind=kLoop, calls=%fused_computation.31 | loop fusion | flops 616320 | bytes 1191552 | tf_op jit(solution)/shard_map/sub | solution.py:23
  28.2 0.0 copy-done.3
  28.2 0.0 copy-done.4
  28.2 0.0 copy-done.5
  28.2 1.4 %fusion.24 = (bf16[64,5136]{1,0:T(8,128)(2,1)}, bf16[64,5136]{1,0:T(8,128)(2,1)}) fusion(f32[8,5136]{1,0:T(8,128)S(1)} %get-tuple-element.36, f32[8,5136]{1,0:T(8,128)S(1)} %copy-done.5, f32[8,5136]{1,0:T(8,128)S(1)} %copy-done.3, f32[8,5136]{1,0:T(8,128)S(1)} %copy-done.4), kind=kLoop, calls=%fused_computation.28 | loop fusion | flops 2629632 | bytes 1972224 | tf_op jit(solution)/shard_map/convert_element_type | solution.py:35
  29.6 15.0 %all-to-all-done = bf16[8,40,2,2,1280]{4,3,2,1,0:T(2,128)(2,1)S(1)} async-done(((bf16[8,40,2,2,1280]{4,3,2,1,0:T(2,128)(2,1)}), bf16[8,40,2,2,1280]{4,3,2,1,0:T(2,128)(2,1)S(1)}, u32[]{:S(2)}, u32[]{:S(2)}) %all-to-all-start) | async-done | bytes 3276832 | tf_op jit(solution)/shard_map/all_to_all | solution.py:62
  44.6 5.0 %fusion.20 = f32[40,2,8,2,32]{4,2,3,1,0:T(8,128)} fusion(bf16[8,40,2,2,1280]{4,3,2,1,0:T(2,128)(2,1)S(1)} %all-to-all-done, bf16[40,16,1280]{2,1,0:T(8,128)(2,1)} %get-tuple-element.17, bf16[40,16,1280]{2,1,0:T(8,128)(2,1)} %get-tuple-element.16), kind=kOutput, calls=%fused_computation.25 | convolution fusion | flops 111411200 | bytes 6717440 | tf_op jit(solution)/shard_map/lscfk,sjk->sclfj/dot_general | solution.py:74
  49.6 0.0 copy-start.1
  49.6 0.0 copy-start
  49.6 1.5 %copy.14 = f32[40,2,8,2,32]{0,4,3,2,1:T(8,128)S(1)} copy(f32[40,2,8,2,32]{4,2,3,1,0:T(8,128)} %fusion.20) | data formatting | bytes 327680 | tf_op jit(solution)/shard_map/lscfk,sjk->sclfj/transpose | solution.py:74
  51.1 0.6 fusion.23
  51.7 0.1 copy.15
  51.9 1.0 %reshape.476 = bf16[32,2,640]{2,1,0:T(2,128)(2,1)} reshape(bf16[32,1,2,16,40]{4,3,2,1,0:T(8,128)(2,1)S(1)} %bitcast.84) | data formatting | bytes 163840
  52.9 4.0 %all-to-all-start.1 = ((bf16[32,2,640]{2,1,0:T(2,128)(2,1)}), bf16[32,2,640]{2,1,0:T(2,128)(2,1)S(1)}, u32[]{:S(2)}, u32[]{:S(2)}) async-start(bf16[32,2,640]{2,1,0:T(2,128)(2,1)} %reshape.476), calls=%async_computation.1 | async-start | bytes 163840 | tf_op jit(solution)/shard_map/all_to_all | solution.py:94
  56.9 0.6 select_multiply_fusion
  57.5 0.0 copy-done.1
  57.5 1.3 %copy.17 = bf16[64,5136]{0,1:T(8,128)(2,1)S(1)} copy(bf16[64,5136]{1,0:T(8,128)(2,1)S(1)} %copy-done.1) | data formatting | bytes 1314816 | tf_op jit(solution)/shard_map/convert_element_type | solution.py:35
  58.8 0.0 copy-done
  58.9 0.0 copy-start.9
  58.9 1.3 %copy.18 = bf16[64,5136]{0,1:T(8,128)(2,1)S(1)} copy(bf16[64,5136]{1,0:T(8,128)(2,1)S(1)} %copy-done) | data formatting | bytes 1314816 | tf_op jit(solution)/shard_map/convert_element_type | solution.py:36
  60.2 1.2 %add.119 = f32[20,5136]{1,0:T(8,128)S(1)} reshape(f32[5,4,5136]{2,1,0:T(4,128)} %get-tuple-element.21) | data formatting | bytes 821760 | tf_op jit(solution)/shard_map/add | solution.py:24
  61.3 2.0 %sub.33 = f32[20,5136]{1,0:T(8,128)} reshape(f32[5,4,5136]{2,1,0:T(4,128)} %get-tuple-element.20) | data formatting | bytes 821760 | tf_op jit(solution)/shard_map/sub | solution.py:23
  63.3 0.6 iota_compare_fusion.2
  63.9 0.5 all-to-all-done.1
  64.5 0.4 reshape.477
  64.9 0.1 copy.16
  65.0 0.3 reshape.449
  65.3 0.0 copy-done.9
  65.4 0.7 fusion.14
  66.1 0.1 squeeze.17
  66.3 0.1 squeeze.16
  66.4 0.1 maximum_bitcast_fusion.6
  66.5 0.0 copy-start.2
  66.5 2.4 %fusion.17 = f32[2,16,20,5136]{3,2,1,0:T(8,128)S(1)} fusion(bf16[64,5136]{0,1:T(8,128)(2,1)S(1)} %copy.18, bf16[64,5136]{0,1:T(8,128)(2,1)S(1)} %copy.17, bf16[1,16,20,128]{3,2,1,0:T(8,128)(2,1)S(1)} %get-tuple-element.23, bf16[1,16,20,128]{3,2,1,0:T(8,128)(2,1)S(1)} %get-tuple-element.22), kind=kOutput, calls=%fused_computation.22 | convolution fusion | flops 844193792 | bytes 14626816 | tf_op jit(solution)/shard_map/dfab,bi->dfai/dot_general | solution.py:46
  69.0 0.0 copy-done.2
  69.0 1.8 %fusion.2 = f32[16,5136]{1,0:T(8,128)S(1)} fusion(f32[2,16,20,5136]{3,2,1,0:T(8,128)S(1)} %fusion.17, f32[20,5136]{1,0:T(8,128)S(1)} %add.119, f32[20,5136]{1,0:T(8,128)S(1)} %copy-done.2), kind=kLoop, calls=%fused_computation.3 | loop fusion | flops 6491904 | bytes 14298624 | tf_op jit(solution)/shard_map/reduce_sum | solution.py:47
  70.8 0.2 reduce_sum.12
  71.0 0.2 broadcast_select_fusion.2
  71.1 10.9 %all_to_all.19 = f32[1,8,2,5136]{3,2,0,1:T(2,128)S(1)} all-to-all(f32[1,8,2,5136]{3,2,0,1:T(2,128)S(1)} %broadcast_select_fusion.2), channel_id=1, replica_groups=mesh['wave'=4,'lev'=8] {'lev'}, dimensions={1} | all-to-all | bytes 657408 | tf_op jit(solution)/shard_map/all_to_all | solution.py:117
  82.1 0.7 copy.28
  (9 shorter events, 0.1 us)
Async XLA Ops:
  0.0 5.3 %copy-start.11 = (s32[32]{0:T(128)S(1)}, s32[32]{0:T(128)}, u32[]{:S(2)}) copy-start(s32[32]{0:T(128)} %param.9) | copy-start | bytes 388
  0.0 7.9 %copy-start.10 = (s32[32]{0:T(128)S(1)}, s32[32]{0:T(128)}, u32[]{:S(2)}) copy-start(s32[32]{0:T(128)} %param.8) | copy-start | bytes 388
  0.0 44.6 %all-to-all-start = ((bf16[8,40,2,2,1280]{4,3,2,1,0:T(2,128)(2,1)}), bf16[8,40,2,2,1280]{4,3,2,1,0:T(2,128)(2,1)S(1)}, u32[]{:S(2)}, u32[]{:S(2)}) async-start(bf16[8,40,2,2,1280]{4,3,2,1,0:T(2,128)(2,1)} %bitcast.81), calls=%async_computation | async-start | bytes 6553600 | tf_op jit(solution)/shard_map/all_to_all | solution.py:62
  22.4 4.6 %copy-start.6 = (f32[5,5136]{1,0:T(8,128)S(1)}, f32[5,5136]{1,0:T(8,128)}, u32[]{:S(2)}) copy-start(f32[5,5136]{1,0:T(8,128)} %get-tuple-element.26) | copy-start | bytes 308164
  22.4 4.6 %copy-start.7 = (f32[5,5136]{1,0:T(8,128)S(1)}, f32[5,5136]{1,0:T(8,128)}, u32[]{:S(2)}) copy-start(f32[5,5136]{1,0:T(8,128)} %get-tuple-element.27) | copy-start | bytes 308164
  22.4 4.6 %copy-start.8 = (f32[4,5136]{1,0:T(4,128)S(1)}, f32[4,5136]{1,0:T(4,128)}, u32[]{:S(2)}) copy-start(f32[4,5136]{1,0:T(4,128)} %get-tuple-element.29) | copy-start | bytes 246532
  23.4 4.8 %copy-start.3 = (f32[8,5136]{1,0:T(8,128)S(1)}, f32[8,5136]{1,0:T(8,128)}, u32[]{:S(2)}) copy-start(f32[8,5136]{1,0:T(8,128)} %get-tuple-element.37) | copy-start | bytes 493060
  23.4 4.8 %copy-start.4 = (f32[8,5136]{1,0:T(8,128)S(1)}, f32[8,5136]{1,0:T(8,128)}, u32[]{:S(2)}) copy-start(f32[8,5136]{1,0:T(8,128)} %get-tuple-element.34) | copy-start | bytes 493060
  23.4 4.8 %copy-start.5 = (f32[8,5136]{1,0:T(8,128)S(1)}, f32[8,5136]{1,0:T(8,128)}, u32[]{:S(2)}) copy-start(f32[8,5136]{1,0:T(8,128)} %get-tuple-element.35) | copy-start | bytes 493060
  49.6 7.9 %copy-start.1 = (bf16[64,5136]{1,0:T(8,128)(2,1)S(1)}, bf16[64,5136]{1,0:T(8,128)(2,1)}, u32[]{:S(2)}) copy-start(bf16[64,5136]{1,0:T(8,128)(2,1)} %get-tuple-element.18) | copy-start | bytes 1972228
  49.6 9.3 %copy-start = (bf16[64,5136]{1,0:T(8,128)(2,1)S(1)}, bf16[64,5136]{1,0:T(8,128)(2,1)}, u32[]{:S(2)}) copy-start(bf16[64,5136]{1,0:T(8,128)(2,1)} %get-tuple-element.19) | copy-start | bytes 1972228
  52.9 11.6 %all-to-all-start.1 = ((bf16[32,2,640]{2,1,0:T(2,128)(2,1)}), bf16[32,2,640]{2,1,0:T(2,128)(2,1)S(1)}, u32[]{:S(2)}, u32[]{:S(2)}) async-start(bf16[32,2,640]{2,1,0:T(2,128)(2,1)} %reshape.476), calls=%async_computation.1 | async-start | bytes 163840 | tf_op jit(solution)/shard_map/all_to_all | solution.py:94
  58.9 6.5 %copy-start.9 = (s32[1280]{0:T(1024)S(1)}, s32[1280]{0:T(1024)}, u32[]{:S(2)}) copy-start(s32[1280]{0:T(1024)} %param.7) | copy-start | bytes 15364
  66.5 2.4 %copy-start.2 = (f32[20,5136]{1,0:T(8,128)S(1)}, f32[20,5136]{1,0:T(8,128)}, u32[]{:S(2)}) copy-start(f32[20,5136]{1,0:T(8,128)} %sub.33) | copy-start | bytes 1232644
where the time goes:
time: 83.3 us; the launch traced here: 82.8 us
  other arithmetic  22.5 us (27%)
  waiting for transfers between devices  15.5 us (19%)
  local copies, waits for them, and re-layouts  11.6 us (14%)
  blocking collectives  10.9 us (13%)
  starting transfers between devices  9.3 us (11%)
  matrix products  8.76 us (11%)
  between operations  4.15 us (5%)
    all_to_all x1, waiting for transfers between devices, on_device(): lax.all_to_all(spec_v, ('lev_g', 'lev_r'), split_axis=0, concat_axis=0, t...  15 us
    all_to_all x1, blocking collectives, on_device(): lax.all_to_all(grid, 'lev_r', split_axis=1, concat_axis=0, tiled=True)  10.9 us
    cos x3, other arithmetic, trig_pair(): return (jnp.cos(theta), jnp.sin(theta))  9.06 us
    all_to_all x1, starting transfers between devices, on_device(): lax.all_to_all(spec_v, ('lev_g', 'lev_r'), split_axis=0, concat_axis=0, t...  5.3 us
    dot_general x1, matrix products, on_device(): jnp.einsum('lscfk,sjk->sclfj', gathered, leg2, preferred_element_type=jnp...  4.99 us
    all_to_all x1, starting transfers between devices, on_device(): lax.all_to_all(fourier, ('wave', 'lev_g', 'lev_r'), split_axis=0, concat_...  4 us
    select_n x1, other arithmetic, on_device(): jnp.where(even_mask, legendre, zeros)  3.64 us
    sin x1, other arithmetic, trig_pair(): return (jnp.cos(theta), jnp.sin(theta))  2.94 us
  transfers between devices with their start and end apart: 2, of which 2 were waited for; matrix products, arithmetic and copies ran while one was open for 33% of the time, Pallas kernels for 0%

commit v1 on v0

--- a/solution.py
+++ b/solution.py
@@ -114,7 +114,10 @@
     lon = grid.shape[-1]
     fpd = fpg // n_r
     grid = grid.reshape(rows_per_dev, n_r, fpd, lon)
-    grid = lax.all_to_all(grid, "lev_r", split_axis=1, concat_axis=0, tiled=True)
+    size = lax.axis_size("lev_r")
+    tiles = jnp.stack(jnp.split(grid, size, axis=1), axis=0)
+    tiles = lax.all_to_all(tiles, "lev_r", split_axis=0, concat_axis=0)
+    grid = jnp.concatenate(tiles, axis=0)
     return grid.reshape(n_r * rows_per_dev, fpd, lon)
 
 

time: 83.3 us -> 83.4 us (level)
    unnamed x27 -> x34, local copies, waits for them, and re-layouts: 2.18 us -> 2.25 us
where the time goes in v1:
time: 83.4 us; the launch traced here: 82.9 us
  other arithmetic  22.5 us (27%)
  waiting for transfers between devices  15.5 us (19%)
  local copies, waits for them, and re-layouts  11.7 us (14%)
  blocking collectives  10.9 us (13%)
  starting transfers between devices  9.3 us (11%)
  matrix products  8.76 us (11%)
  between operations  4.2 us (5%)
    all_to_all x1, waiting for transfers between devices, on_device(): lax.all_to_all(spec_v, ('lev_g', 'lev_r'), split_axis=0, concat_axis=0, t...  15 us
    all_to_all x1, blocking collectives, on_device(): tiles = lax.all_to_all(tiles, 'lev_r', split_axis=0, concat_axis=0)  10.9 us
    cos x3, other arithmetic, trig_pair(): return (jnp.cos(theta), jnp.sin(theta))  9.06 us
    all_to_all x1, starting transfers between devices, on_device(): lax.all_to_all(spec_v, ('lev_g', 'lev_r'), split_axis=0, concat_axis=0, t...  5.3 us
    dot_general x1, matrix products, on_device(): jnp.einsum('lscfk,sjk->sclfj', gathered, leg2, preferred_element_type=jnp...  4.99 us
    all_to_all x1, starting transfers between devices, on_device(): lax.all_to_all(fourier, ('wave', 'lev_g', 'lev_r'), split_axis=0, concat_...  4 us
    select_n x1, other arithmetic, on_device(): jnp.where(even_mask, legendre, zeros)  3.64 us
    sin x1, other arithmetic, trig_pair(): return (jnp.cos(theta), jnp.sin(theta))  2.94 us
  transfers between devices with their start and end apart: 2, of which 2 were waited for; matrix products, arithmetic and copies ran while one was open for 33% of the time, Pallas kernels for 0%

profile of v1, /device:TPU:0, one launch (start us, length us, event | category | flops | bytes accessed | tf_op | source)
XLA Modules:
  0.0 82.9 jit_solution(17707785176414112282)
XLA Ops:
  0.0 0.0 copy-start.11
  0.0 0.0 copy-start.10
  0.0 5.3 %all-to-all-start = ((bf16[8,40,2,2,1280]{4,3,2,1,0:T(2,128)(2,1)}), bf16[8,40,2,2,1280]{4,3,2,1,0:T(2,128)(2,1)S(1)}, u32[]{:S(2)}, u32[]{:S(2)}) async-start(bf16[8,40,2,2,1280]{4,3,2,1,0:T(2,128)(2,1)} %bitcast.113), calls=%async_computation | async-start | bytes 6553600 | tf_op jit(solution)/shard_map/all_to_all | solution.py:62
  5.3 0.0 copy-done.11
  5.4 0.6 dynamic_slice.6
  7.9 0.0 copy-done.10
  7.9 0.6 dynamic-slice.2
  10.4 2.9 %fusion.61 = (f32[8,5136]{1,0:T(8,128)S(1)}, f32[8,5136]{1,0:T(8,128)}) fusion(f32[]{:T(128)S(6)} %convert_element_type.83, pred[]{:T(512)S(6)} %lt.109, s32[]{:T(128)S(6)} %select_n.155), kind=kLoop, calls=%fused_computation.79 | loop fusion | flops 451968 | bytes 328713 | tf_op jit(solution)/shard_map/sin | solution.py:17
  13.4 3.1 %fusion.64 = (f32[8,5136]{1,0:T(8,128)}, f32[8,5136]{1,0:T(8,128)}) fusion(f32[]{:T(128)S(6)} %convert_element_type.83, pred[]{:T(512)S(6)} %lt.109, s32[]{:T(128)S(6)} %select_n.155, s32[8]{0:T(128)S(1)} %iota_multiply_fusion.2), kind=kLoop, calls=%fused_computation.82 | loop fusion | flops 451968 | bytes 328745 | tf_op jit(solution)/shard_map/cos | solution.py:17
  16.4 3.0 %fusion.60 = (f32[5,5136]{1,0:T(8,128)}, f32[5,5136]{1,0:T(8,128)}) fusion(f32[]{:T(128)S(6)} %convert_element_type.83, pred[]{:T(512)S(6)} %lt.109, s32[]{:T(128)S(6)} %select_n.155, s32[5]{0:T(128)S(1)} %iota_multiply_fusion.1), kind=kLoop, calls=%fused_computation.78 | loop fusion | flops 282480 | bytes 205469 | tf_op jit(solution)/shard_map/cos | solution.py:17
  19.5 3.0 %fusion.74 = (f32[4,5136]{1,0:T(4,128)S(1)}, f32[4,5136]{1,0:T(4,128)}) fusion(f32[]{:T(128)S(6)} %convert_element_type.83, pred[]{:T(512)S(6)} %lt.109, s32[]{:T(128)S(6)} %select_n.155, s32[4]{0:T(128)S(1)} %iota_multiply_fusion), kind=kLoop, calls=%fused_computation.100 | loop fusion | flops 225984 | bytes 164377 | tf_op jit(solution)/shard_map/cos | solution.py:17
  22.4 0.0 copy-start.6
  22.4 0.0 copy-start.7
  22.4 0.0 copy-start.8
  22.4 0.8 dynamic-slice_subtract_fusion
  23.3 0.1 fusion.27
  23.4 0.0 copy-start.3
  23.4 0.0 copy-start.4
  23.4 0.0 copy-start.5
  23.4 3.6 %broadcast_select_fusion.1 = (bf16[40,16,1280]{2,1,0:T(8,128)(2,1)}, bf16[40,16,1280]{2,1,0:T(8,128)(2,1)}) fusion(bf16[40,16,1280]{2,1,0:T(8,128)(2,1)} %param.6, pred[40,1280]{1,0:T(8,128)(4,1)S(1)} %get-tuple-element.32, pred[40,1280]{1,0:T(8,128)(4,1)S(1)} %get-tuple-element.33), kind=kLoop, calls=%fused_computation.18 | loop fusion | flops 1638400 | bytes 5017600 | tf_op jit(solution)/shard_map/jit(_where)/select_n | solution.py:72
  27.1 0.0 copy-done.6
  27.1 0.0 copy-done.7
  27.1 0.0 copy-done.8
  27.1 1.1 %multiply_subtract_fusion = (f32[5,4,5136]{2,1,0:T(4,128)}, f32[5,4,5136]{2,1,0:T(4,128)}) fusion(f32[4,5136]{1,0:T(4,128)S(1)} %copy-done.8, f32[5,5136]{1,0:T(8,128)S(1)} %copy-done.7, f32[4,5136]{1,0:T(4,128)S(1)} %get-tuple-element.28, f32[5,5136]{1,0:T(8,128)S(1)} %copy-done.6), kind=kLoop, calls=%fused_computation.31 | loop fusion | flops 616320 | bytes 1191552 | tf_op jit(solution)/shard_map/sub | solution.py:23
  28.2 0.0 copy-done.3
  28.2 0.0 copy-done.4
  28.2 0.0 copy-done.5
  28.2 1.4 %fusion.24 = (bf16[64,5136]{1,0:T(8,128)(2,1)}, bf16[64,5136]{1,0:T(8,128)(2,1)}) fusion(f32[8,5136]{1,0:T(8,128)S(1)} %get-tuple-element.36, f32[8,5136]{1,0:T(8,128)S(1)} %copy-done.5, f32[8,5136]{1,0:T(8,128)S(1)} %copy-done.3, f32[8,5136]{1,0:T(8,128)S(1)} %copy-done.4), kind=kLoop, calls=%fused_computation.28 | loop fusion | flops 2629632 | bytes 1972224 | tf_op jit(solution)/shard_map/convert_element_type | solution.py:35
  29.6 15.0 %all-to-all-done = bf16[8,40,2,2,1280]{4,3,2,1,0:T(2,128)(2,1)S(1)} async-done(((bf16[8,40,2,2,1280]{4,3,2,1,0:T(2,128)(2,1)}), bf16[8,40,2,2,1280]{4,3,2,1,0:T(2,128)(2,1)S(1)}, u32[]{:S(2)}, u32[]{:S(2)}) %all-to-all-start) | async-done | bytes 3276832 | tf_op jit(solution)/shard_map/all_to_all | solution.py:62
  44.6 5.0 %fusion.20 = f32[40,2,8,2,32]{4,2,3,1,0:T(8,128)} fusion(bf16[8,40,2,2,1280]{4,3,2,1,0:T(2,128)(2,1)S(1)} %all-to-all-done, bf16[40,16,1280]{2,1,0:T(8,128)(2,1)} %get-tuple-element.17, bf16[40,16,1280]{2,1,0:T(8,128)(2,1)} %get-tuple-element.16), kind=kOutput, calls=%fused_computation.25 | convolution fusion | flops 111411200 | bytes 6717440 | tf_op jit(solution)/shard_map/lscfk,sjk->sclfj/dot_general | solution.py:74
  49.6 0.0 copy-start.1
  49.6 0.0 copy-start
  49.6 1.5 %copy.28 = f32[40,2,8,2,32]{0,4,3,2,1:T(8,128)S(1)} copy(f32[40,2,8,2,32]{4,2,3,1,0:T(8,128)} %fusion.20) | data formatting | bytes 327680 | tf_op jit(solution)/shard_map/lscfk,sjk->sclfj/transpose | solution.py:74
  51.1 0.6 fusion.23
  51.7 0.1 copy.29
  51.9 1.0 %reshape.468 = bf16[32,2,640]{2,1,0:T(2,128)(2,1)} reshape(bf16[32,1,2,16,40]{4,3,2,1,0:T(8,128)(2,1)S(1)} %bitcast.116) | data formatting | bytes 163840
  52.9 4.0 %all-to-all-start.1 = ((bf16[32,2,640]{2,1,0:T(2,128)(2,1)}), bf16[32,2,640]{2,1,0:T(2,128)(2,1)S(1)}, u32[]{:S(2)}, u32[]{:S(2)}) async-start(bf16[32,2,640]{2,1,0:T(2,128)(2,1)} %reshape.468), calls=%async_computation.1 | async-start | bytes 163840 | tf_op jit(solution)/shard_map/all_to_all | solution.py:94
  56.9 0.6 select_multiply_fusion
  57.5 0.0 copy-done.1
  57.5 1.3 %copy.31 = bf16[64,5136]{0,1:T(8,128)(2,1)S(1)} copy(bf16[64,5136]{1,0:T(8,128)(2,1)S(1)} %copy-done.1) | data formatting | bytes 1314816 | tf_op jit(solution)/shard_map/convert_element_type | solution.py:35
  58.8 0.0 copy-done
  58.9 0.0 copy-start.9
  58.9 1.3 %copy.32 = bf16[64,5136]{0,1:T(8,128)(2,1)S(1)} copy(bf16[64,5136]{1,0:T(8,128)(2,1)S(1)} %copy-done) | data formatting | bytes 1314816 | tf_op jit(solution)/shard_map/convert_element_type | solution.py:36
  60.2 1.2 %add.119 = f32[20,5136]{1,0:T(8,128)S(1)} reshape(f32[5,4,5136]{2,1,0:T(4,128)} %get-tuple-element.21) | data formatting | bytes 821760 | tf_op jit(solution)/shard_map/add | solution.py:24
  61.3 2.0 %sub.33 = f32[20,5136]{1,0:T(8,128)} reshape(f32[5,4,5136]{2,1,0:T(4,128)} %get-tuple-element.20) | data formatting | bytes 821760 | tf_op jit(solution)/shard_map/sub | solution.py:23
  63.3 0.6 iota_compare_fusion.2
  63.9 0.5 all-to-all-done.1
  64.5 0.4 reshape.469
  64.9 0.1 copy.30
  65.0 0.3 reshape.442
  65.3 0.0 copy-done.9
  65.4 0.7 fusion.14
  66.1 0.1 squeeze.17
  66.3 0.1 squeeze.16
  66.4 0.1 maximum_bitcast_fusion.6
  66.5 0.0 copy-start.2
  66.5 2.4 %fusion.17 = f32[2,16,20,5136]{3,2,1,0:T(8,128)S(1)} fusion(bf16[64,5136]{0,1:T(8,128)(2,1)S(1)} %copy.32, bf16[64,5136]{0,1:T(8,128)(2,1)S(1)} %copy.31, bf16[1,16,20,128]{3,2,1,0:T(8,128)(2,1)S(1)} %get-tuple-element.23, bf16[1,16,20,128]{3,2,1,0:T(8,128)(2,1)S(1)} %get-tuple-element.22), kind=kOutput, calls=%fused_computation.22 | convolution fusion | flops 844193792 | bytes 14626816 | tf_op jit(solution)/shard_map/dfab,bi->dfai/dot_general | solution.py:46
  69.0 0.0 copy-done.2
  69.0 1.8 %fusion.2 = f32[16,5136]{1,0:T(8,128)S(1)} fusion(f32[2,16,20,5136]{3,2,1,0:T(8,128)S(1)} %fusion.17, f32[20,5136]{1,0:T(8,128)S(1)} %add.119, f32[20,5136]{1,0:T(8,128)S(1)} %copy-done.2), kind=kLoop, calls=%fused_computation.3 | loop fusion | flops 6491904 | bytes 14298624 | tf_op jit(solution)/shard_map/reduce_sum | solution.py:47
  70.8 0.2 reduce_sum.12
  71.0 0.2 broadcast_select_fusion.2
  71.3 10.9 %all_to_all.15 = f32[8,1,1,2,5136]{4,3,2,1,0:T(2,128)S(1)} all-to-all(f32[8,1,1,2,5136]{4,3,2,1,0:T(2,128)S(1)} %fusion.65), channel_id=1, replica_groups=mesh['wave'=4,'lev'=8] {'lev'}, dimensions={0} | all-to-all | bytes 657408 | tf_op jit(solution)/shard_map/all_to_all | solution.py:119
  82.2 0.7 copy.49
  (17 shorter events, 0.2 us)
Async XLA Ops:
  0.0 5.3 %copy-start.11 = (s32[32]{0:T(128)S(1)}, s32[32]{0:T(128)}, u32[]{:S(2)}) copy-start(s32[32]{0:T(128)} %param.9) | copy-start | bytes 388
  0.0 7.9 %copy-start.10 = (s32[32]{0:T(128)S(1)}, s32[32]{0:T(128)}, u32[]{:S(2)}) copy-start(s32[32]{0:T(128)} %param.8) | copy-start | bytes 388
  0.0 44.6 %all-to-all-start = ((bf16[8,40,2,2,1280]{4,3,2,1,0:T(2,128)(2,1)}), bf16[8,40,2,2,1280]{4,3,2,1,0:T(2,128)(2,1)S(1)}, u32[]{:S(2)}, u32[]{:S(2)}) async-start(bf16[8,40,2,2,1280]{4,3,2,1,0:T(2,128)(2,1)} %bitcast.113), calls=%async_computation | async-start | bytes 6553600 | tf_op jit(solution)/shard_map/all_to_all | solution.py:62
  22.4 4.6 %copy-start.6 = (f32[5,5136]{1,0:T(8,128)S(1)}, f32[5,5136]{1,0:T(8,128)}, u32[]{:S(2)}) copy-start(f32[5,5136]{1,0:T(8,128)} %get-tuple-element.26) | copy-start | bytes 308164
  22.4 4.6 %copy-start.7 = (f32[5,5136]{1,0:T(8,128)S(1)}, f32[5,5136]{1,0:T(8,128)}, u32[]{:S(2)}) copy-start(f32[5,5136]{1,0:T(8,128)} %get-tuple-element.27) | copy-start | bytes 308164
  22.4 4.6 %copy-start.8 = (f32[4,5136]{1,0:T(4,128)S(1)}, f32[4,5136]{1,0:T(4,128)}, u32[]{:S(2)}) copy-start(f32[4,5136]{1,0:T(4,128)} %get-tuple-element.29) | copy-start | bytes 246532
  23.4 4.8 %copy-start.3 = (f32[8,5136]{1,0:T(8,128)S(1)}, f32[8,5136]{1,0:T(8,128)}, u32[]{:S(2)}) copy-start(f32[8,5136]{1,0:T(8,128)} %get-tuple-element.37) | copy-start | bytes 493060
  23.4 4.8 %copy-start.4 = (f32[8,5136]{1,0:T(8,128)S(1)}, f32[8,5136]{1,0:T(8,128)}, u32[]{:S(2)}) copy-start(f32[8,5136]{1,0:T(8,128)} %get-tuple-element.34) | copy-start | bytes 493060
  23.4 4.8 %copy-start.5 = (f32[8,5136]{1,0:T(8,128)S(1)}, f32[8,5136]{1,0:T(8,128)}, u32[]{:S(2)}) copy-start(f32[8,5136]{1,0:T(8,128)} %get-tuple-element.35) | copy-start | bytes 493060
  49.6 7.9 %copy-start.1 = (bf16[64,5136]{1,0:T(8,128)(2,1)S(1)}, bf16[64,5136]{1,0:T(8,128)(2,1)}, u32[]{:S(2)}) copy-start(bf16[64,5136]{1,0:T(8,128)(2,1)} %get-tuple-element.18) | copy-start | bytes 1972228
  49.6 9.3 %copy-start = (bf16[64,5136]{1,0:T(8,128)(2,1)S(1)}, bf16[64,5136]{1,0:T(8,128)(2,1)}, u32[]{:S(2)}) copy-start(bf16[64,5136]{1,0:T(8,128)(2,1)} %get-tuple-element.19) | copy-start | bytes 1972228
  52.9 11.6 %all-to-all-start.1 = ((bf16[32,2,640]{2,1,0:T(2,128)(2,1)}), bf16[32,2,640]{2,1,0:T(2,128)(2,1)S(1)}, u32[]{:S(2)}, u32[]{:S(2)}) async-start(bf16[32,2,640]{2,1,0:T(2,128)(2,1)} %reshape.468), calls=%async_computation.1 | async-start | bytes 163840 | tf_op jit(solution)/shard_map/all_to_all | solution.py:94
  58.9 6.5 %copy-start.9 = (s32[1280]{0:T(1024)S(1)}, s32[1280]{0:T(1024)}, u32[]{:S(2)}) copy-start(s32[1280]{0:T(1024)} %param.7) | copy-start | bytes 15364
  66.5 2.4 %copy-start.2 = (f32[20,5136]{1,0:T(8,128)S(1)}, f32[20,5136]{1,0:T(8,128)}, u32[]{:S(2)}) copy-start(f32[20,5136]{1,0:T(8,128)} %sub.33) | copy-start | bytes 1232644
